TPU v7x, 512 devices: a whole 4x8x8 slice. The times are simulated.
512 devices in a mesh: ind: 64 (over y, z), snp: 8 (over x, core).
Axes of the slice: x: 4, y: 8, z: 8, core: 2. Of those that a mesh axis runs over, the one named last changes fastest.
Arguments:
- genotypes: int32 [4096, 16384], P('ind', 'snp'), may hold values from 0 to 2
- observed: int32 [4096, 16384], P('ind', 'snp'), may hold values from 0 to 1
- ancestry: float32 [4096, 32], P('ind'), may hold values from 0.018 to 54.6, as said below
- freqs: float32 [16384, 32], P(('snp', 'ind')), may hold values from 0.05 to 0.95
Outputs:
- ancestry_out: float32 [4096, 32], P('ind')
- freqs_out: float32 [16384, 32], P(('snp', 'ind'))
Inputs may be any that keep to these rules, and one draw needn't show every extreme that they name: `ancestry`: positive weights.
All inputs are finite; a program needn't handle non-finite values.
Results may differ from a plain program's by a relative error of at most 0.0003.
Values sent between devices are 32-bit elements; how exact they have to be, the bound alone decides.
No kernel may reach another device: no remote copies, remote signals or barrier semaphores. Data moves between devices by JAX's collectives and lax.ppermute only.
A program may use at most 64 MiB of HBM per device.

v0:
```python
import jax
import jax.numpy as jnp
from jax import lax
from jax.sharding import PartitionSpec as P

STEPS = 3
clip_low = 1e-05
high = lax.Precision.HIGHEST


def over_rows(left, right):
    return lax.dot_general(
        left, right, (((0,), (0,)), ((), ())), precision=high, preferred_element_type=jnp.float32
    )


def per_device(genotypes, observed, ancestry, freqs):
    ind_count = lax.axis_size("ind")
    snp_count = lax.axis_size("snp")
    geno = genotypes.astype(jnp.float32)
    seen = observed.astype(jnp.float32)
    hits = seen * geno
    misses = seen * (2.0 - geno)
    own_rows = freqs.shape[0]
    q_zero = ancestry / jnp.sum(ancestry, axis=1, keepdims=True)
    f_zero = lax.all_gather(freqs, "ind", axis=0, tiled=True)
    f_weight = 1.0 / ind_count
    q_weight = 1.0 / snp_count

    def em_map(q_rows, f_state):
        prob = jnp.dot(q_rows, f_state.T, precision=high, preferred_element_type=jnp.float32)
        ratio_a = hits / prob
        ratio_b = misses / (1.0 - prob)
        sum_a = jnp.dot(ratio_a, f_state, precision=high, preferred_element_type=jnp.float32)
        sum_b = jnp.dot(ratio_b, 1.0 - f_state, precision=high, preferred_element_type=jnp.float32)
        c_part = over_rows(ratio_a, q_rows)
        d_part = over_rows(ratio_b, q_rows)
        sum_a, sum_b = lax.psum((sum_a, sum_b), "snp")
        q_next = q_rows * (sum_a + sum_b)
        q_next = q_next / jnp.sum(q_next, axis=1, keepdims=True)
        c_total, d_total = lax.psum((c_part, d_part), "ind")
        f_next = f_state * c_total / (f_state * c_total + (1.0 - f_state) * d_total)
        return (q_next, f_next)

    for step in range(STEPS):
        q_one, f_one = em_map(q_zero, f_zero)
        rq = q_one - q_zero
        rf = f_one - f_zero
        first_local = q_weight * jnp.sum(rq * rq) + f_weight * jnp.sum(rf * rf)
        q_two, f_two = em_map(q_one, f_one)
        vq = q_two - 2.0 * q_one + q_zero
        vf = f_two - 2.0 * f_one + f_zero
        second_local = q_weight * jnp.sum(vq * vq) + f_weight * jnp.sum(vf * vf)
        first, second = lax.psum((first_local, second_local), ("ind", "snp"))
        alpha = -jnp.sqrt(first / (second + 1e-20))
        q_ext = jnp.clip(q_zero - 2.0 * alpha * rq + alpha * alpha * vq, clip_low, 1.0 - clip_low)
        q_zero = q_ext / jnp.sum(q_ext, axis=1, keepdims=True)
        f_zero = jnp.clip(f_zero - 2.0 * alpha * rf + alpha * alpha * vf, clip_low, 1.0 - clip_low)
    f_final = lax.dynamic_slice_in_dim(f_zero, lax.axis_index("ind") * own_rows, own_rows, 0)
    return (q_zero, f_final)


def solution(mesh):
    in_specs = (P("ind", "snp"), P("ind", "snp"), P("ind", None), P(("snp", "ind"), None))
    out_specs = (P("ind", None), P(("snp", "ind"), None))
    return jax.shard_map(
        per_device, mesh=mesh, in_specs=in_specs, out_specs=out_specs, check_vma=False
    )
```

profile of v0, /device:TPU:1, one launch (start us, length us, event | category | flops | bytes accessed | tf_op | source)
XLA Modules:
  0.0 1308.1 jit_solution(10451656634871468365)
XLA Ops:
  7.2 47.0 %all_gather.3 = f32[2048,32]{1,0:T(8,128)S(1)} all-gather(f32[32,32]{1,0:T(8,128)} %param.7), channel_id=1, replica_groups=mesh['ind'=64,'snp'=8] {'ind'}, dimensions={0}, use_global_device_ids=true | all-gather | bytes 266240 | tf_op jit(solution)/shard_map/all_gather | solution.py:26
  54.3 1.3 fusion.48
  55.6 0.1 convert_multiply_fusion
  55.7 1.2 fusion.46
  56.9 1.2 fusion.45
  58.2 0.0 all-reduce.24.cloned.1.call-start
  58.2 0.3 copy.8
  58.5 0.6 fusion.11
  59.1 1.8 convolution_add_fusion
  60.9 32.1 %psum.240 = f32[64,32]{0,1:T(8,128)S(1)} all-reduce(f32[64,32]{0,1:T(8,128)S(1)} %convolution_add_fusion), channel_id=1, replica_groups=mesh['ind'=64,'snp'=8] {'snp'}, use_global_device_ids=true, to_apply=%region_1.0 | all-reduce | flops 2048 | bytes 16384 | tf_op jit(solution)/shard_map/psum | solution.py:38
  93.0 123.9 %all-reduce.26.cloned.1.call-done = (f32[2048,32]{0,1:T(8,128)}, f32[2048,32]{0,1:T(8,128)}) async-done(((f32[2048,32]{0,1:T(8,128)}, f32[2048,32]{0,1:T(8,128)}), (f32[2048,32]{0,1:T(8,128)}, f32[2048,32]{0,1:T(8,128)})) %all-reduce.26.cloned.1.call-update) | async-done | bytes 524304 | tf_op jit(solution)/shard_map/psum | solution.py:41
  216.9 1.7 multiply_reduce_fusion.5
  218.6 0.6 fusion.30
  219.2 1.2 fusion.27
  220.4 1.2 fusion.28
  221.7 0.6 fusion.72
  222.3 0.6 convolution_add_fusion.5
  222.9 24.9 %psum.241 = f32[64,32]{0,1:T(8,128)S(1)} all-reduce(f32[64,32]{0,1:T(8,128)S(1)} %convolution_add_fusion.5), channel_id=1, replica_groups=mesh['ind'=64,'snp'=8] {'snp'}, use_global_device_ids=true, to_apply=%region_9.0 | all-reduce | flops 2048 | bytes 16384 | tf_op jit(solution)/shard_map/psum | solution.py:38
  247.8 0.7 multiply_reduce_fusion.10
  250.5 123.8 %all-reduce.24.cloned.1.call-done = (f32[2048,32]{0,1:T(8,128)}, f32[2048,32]{0,1:T(8,128)}) async-done(((f32[2048,32]{0,1:T(8,128)}, f32[2048,32]{0,1:T(8,128)}), (f32[2048,32]{0,1:T(8,128)}, f32[2048,32]{0,1:T(8,128)})) %all-reduce.24.cloned.1.call-update) | async-done | bytes 524304 | tf_op jit(solution)/shard_map/psum | solution.py:41
  374.3 1.7 multiply_reduce_fusion.4
  376.7 99.3 %all-reduce.2 = (f32[]{:T(128)}, f32[]{:T(128)}) all-reduce(f32[]{:T(128)S(6)} %add.164, f32[]{:T(128)S(6)} %add.169), channel_id=1, replica_groups=mesh['ind'=64,'snp'=8] {'ind','snp'}, use_global_device_ids=true, to_apply=%region_8.0 | all-reduce | flops 2 | bytes 16 | tf_op jit(solution)/shard_map/psum | solution.py:54
  477.4 0.1 add_clamp_fusion.1
  477.5 0.6 fusion.52
  478.1 1.2 fusion.49
  479.3 1.2 fusion.50
  480.6 0.0 all-reduce.20.cloned.1.call-start
  480.6 0.6 fusion.69
  481.2 0.6 convolution_add_fusion.4
  481.8 20.9 %psum.242 = f32[64,32]{0,1:T(8,128)S(1)} all-reduce(f32[64,32]{0,1:T(8,128)S(1)} %convolution_add_fusion.4), channel_id=1, replica_groups=mesh['ind'=64,'snp'=8] {'snp'}, use_global_device_ids=true, to_apply=%region_18.19 | all-reduce | flops 2048 | bytes 16384 | tf_op jit(solution)/shard_map/psum | solution.py:38
  502.7 125.4 %all-reduce.22.cloned.1.call-done = (f32[2048,32]{0,1:T(8,128)}, f32[2048,32]{0,1:T(8,128)}) async-done(((f32[2048,32]{0,1:T(8,128)}, f32[2048,32]{0,1:T(8,128)}), (f32[2048,32]{0,1:T(8,128)}, f32[2048,32]{0,1:T(8,128)})) %all-reduce.22.cloned.1.call-update) | async-done | bytes 524304 | tf_op jit(solution)/shard_map/psum | solution.py:41
  628.1 1.7 multiply_reduce_fusion.3
  629.8 0.6 fusion.36
  630.4 1.2 fusion.33
  631.7 1.2 fusion.34
  633.0 0.6 fusion.66
  634.2 0.6 convolution_add_fusion.3
  634.8 24.9 %psum.243 = f32[64,32]{0,1:T(8,128)S(1)} all-reduce(f32[64,32]{0,1:T(8,128)S(1)} %convolution_add_fusion.3), channel_id=1, replica_groups=mesh['ind'=64,'snp'=8] {'snp'}, use_global_device_ids=true, to_apply=%region_26.27 | all-reduce | flops 2048 | bytes 16384 | tf_op jit(solution)/shard_map/psum | solution.py:38
  659.7 0.6 multiply_reduce_fusion.8
  661.6 123.9 %all-reduce.20.cloned.1.call-done = (f32[2048,32]{0,1:T(8,128)}, f32[2048,32]{0,1:T(8,128)}) async-done(((f32[2048,32]{0,1:T(8,128)}, f32[2048,32]{0,1:T(8,128)}), (f32[2048,32]{0,1:T(8,128)}, f32[2048,32]{0,1:T(8,128)})) %all-reduce.20.cloned.1.call-update) | async-done | bytes 524304 | tf_op jit(solution)/shard_map/psum | solution.py:41
  785.6 1.7 multiply_reduce_fusion.2
  787.9 99.4 %all-reduce.1 = (f32[]{:T(128)}, f32[]{:T(128)}) all-reduce(f32[]{:T(128)S(6)} %add.175, f32[]{:T(128)S(6)} %add.180), channel_id=1, replica_groups=mesh['ind'=64,'snp'=8] {'ind','snp'}, use_global_device_ids=true, to_apply=%region_25.26 | all-reduce | flops 2 | bytes 16 | tf_op jit(solution)/shard_map/psum | solution.py:54
  888.7 0.1 add_clamp_fusion
  888.7 0.6 fusion.56
  889.4 1.2 fusion.53
  890.6 1.2 fusion.54
  891.9 0.6 fusion.63
  892.5 0.6 convolution_add_fusion.2
  893.1 20.8 %psum.244 = f32[64,32]{0,1:T(8,128)S(1)} all-reduce(f32[64,32]{0,1:T(8,128)S(1)} %convolution_add_fusion.2), channel_id=1, replica_groups=mesh['ind'=64,'snp'=8] {'snp'}, use_global_device_ids=true, to_apply=%region_35.36 | all-reduce | flops 2048 | bytes 16384 | tf_op jit(solution)/shard_map/psum | solution.py:38
  913.9 125.4 %all-reduce.18.cloned.1.call-done = (f32[2048,32]{0,1:T(8,128)}, f32[2048,32]{0,1:T(8,128)}) async-done(((f32[2048,32]{0,1:T(8,128)}, f32[2048,32]{0,1:T(8,128)}), (f32[2048,32]{0,1:T(8,128)}, f32[2048,32]{0,1:T(8,128)})) %all-reduce.18.cloned.1.call-update) | async-done | bytes 524304 | tf_op jit(solution)/shard_map/psum | solution.py:41
  1039.3 1.7 multiply_reduce_fusion.1
  1041.0 0.6 fusion.42
  1041.6 1.2 fusion.40
  1042.9 1.2 fusion.39
  1044.1 0.6 fusion.60
  1045.3 0.6 convolution_add_fusion.1
  1045.9 24.9 %psum.245 = f32[64,32]{0,1:T(8,128)S(1)} all-reduce(f32[64,32]{0,1:T(8,128)S(1)} %convolution_add_fusion.1), channel_id=1, replica_groups=mesh['ind'=64,'snp'=8] {'snp'}, use_global_device_ids=true, to_apply=%region_43.44 | all-reduce | flops 2048 | bytes 16384 | tf_op jit(solution)/shard_map/psum | solution.py:38
  1070.9 0.6 multiply_reduce_fusion.6
  1072.8 124.0 %all-reduce.16.cloned.1.call-done = (f32[2048,32]{0,1:T(8,128)}, f32[2048,32]{0,1:T(8,128)}) async-done(((f32[2048,32]{0,1:T(8,128)}, f32[2048,32]{0,1:T(8,128)}), (f32[2048,32]{0,1:T(8,128)}, f32[2048,32]{0,1:T(8,128)})) %all-reduce.16.cloned.1.call-update) | async-done | bytes 524304 | tf_op jit(solution)/shard_map/psum | solution.py:41
  1196.8 1.7 multiply_reduce_fusion
  1199.2 99.3 %all-reduce = (f32[]{:T(128)}, f32[]{:T(128)}) all-reduce(f32[]{:T(128)S(6)} %add.186, f32[]{:T(128)S(6)} %add.191), channel_id=1, replica_groups=mesh['ind'=64,'snp'=8] {'ind','snp'}, use_global_device_ids=true, to_apply=%region_42.43 | all-reduce | flops 2 | bytes 16 | tf_op jit(solution)/shard_map/psum | solution.py:54
  1299.9 0.1 fusion.20
  1300.0 0.7 copy.13
  1300.7 0.6 broadcast_divide_fusion
  (26 shorter events, 0.6 us)
Async XLA Ops:
  7.2 47.0 %copy-start.2 = (f32[64,32]{0,1:T(8,128)S(1)}, f32[64,32]{0,1:T(8,128)}, u32[]{:S(2)}) copy-start(f32[64,32]{0,1:T(8,128)} %param.6) | copy-start | bytes 24580
  7.2 209.7 %all-reduce.26.cloned.1.call-start = ((), (), s32[]{:S(2)}) async-start(), calls=%async_computation.5 | async-start | bytes 1048576 | tf_op jit(solution)/shard_map/psum | solution.py:41
  54.2 1.3 copy-start
  54.2 1.3 copy-start.1
  58.2 316.1 %all-reduce.24.cloned.1.call-start = ((), (), s32[]{:S(2)}) async-start(), calls=%async_computation.4 | async-start | bytes 1048576 | tf_op jit(solution)/shard_map/psum | solution.py:41
  221.7 406.4 %all-reduce.22.cloned.1.call-start = ((), (), s32[]{:S(2)}) async-start(), calls=%async_computation.3 | async-start | bytes 1048576 | tf_op jit(solution)/shard_map/psum | solution.py:41
  480.6 305.0 %all-reduce.20.cloned.1.call-start = ((), (), s32[]{:S(2)}) async-start(), calls=%async_computation.2 | async-start | bytes 1048576 | tf_op jit(solution)/shard_map/psum | solution.py:41
  632.9 406.4 %all-reduce.18.cloned.1.call-start = ((), (), s32[]{:S(2)}) async-start(), calls=%async_computation.1 | async-start | bytes 1048576 | tf_op jit(solution)/shard_map/psum | solution.py:41
  891.8 304.9 %all-reduce.16.cloned.1.call-start = ((), (), s32[]{:S(2)}) async-start(), calls=%async_computation | async-start | bytes 1048576 | tf_op jit(solution)/shard_map/psum | solution.py:41
Sparse Core Ops, SparseCore 0:
  58.3 158.5 all-reduce.25
  221.8 152.4 all-reduce.23
  480.7 147.3 all-reduce.21
  633.0 152.4 all-reduce.19
  892.0 147.2 all-reduce.17
  1044.2 152.5 all-reduce.15
where the time goes:
time: 1310 us
  waiting for transfers between devices  746 us (57%)
  blocking collectives  494 us (38%)
  matrix products  27.2 us (2%)
  between operations  26.2 us (2%)
  other arithmetic  13.5 us (1%)
    psum x6, waiting for transfers between devices, em_map(): c_total, d_total = lax.psum((c_part, d_part), 'ind')  746 us
    psum x3, blocking collectives, per_device(): first, second = lax.psum((first_local, second_local), ('ind', 'snp'))  298 us
    psum x6, blocking collectives, em_map(): sum_a, sum_b = lax.psum((sum_a, sum_b), 'snp')  148 us
    all_gather x1, blocking collectives, per_device(): f_zero = lax.all_gather(freqs, 'ind', axis=0, tiled=True)  47 us
  transfers between devices with their start and end apart: 6, of which 6 were waited for; matrix products, arithmetic and copies ran while one was open for 1% of the time, Pallas kernels for 0%

commit v1 on v0

--- a/solution.py
+++ b/solution.py
@@ -23,7 +23,9 @@
     misses = seen * (2.0 - geno)
     own_rows = freqs.shape[0]
     q_zero = ancestry / jnp.sum(ancestry, axis=1, keepdims=True)
-    f_zero = lax.all_gather(freqs, "ind", axis=0, tiled=True)
+    f_zero = jnp.concatenate(
+        lax.all_to_all(jnp.stack([freqs] * lax.axis_size("ind")), "ind", 0, 0), axis=0
+    )
     f_weight = 1.0 / ind_count
     q_weight = 1.0 / snp_count
 

time: 1310 us -> 1280 us (0.977)
  blocking collectives: 494 us -> 438 us
  starting transfers between devices: 0.25 us -> 17.7 us
    all_gather x1 -> x0, blocking collectives: 47 us -> none  [per_device(): f_zero = lax.all_gather(freqs, 'ind', axis=0, tiled=True)]
    all_to_all x0 -> x1, starting transfers between devices: none -> 17.3 us  [per_device(): lax.all_to_all(jnp.stack([freqs] * lax.axis_size('ind')), 'ind', 0, 0)]
  transfers between devices with their start and end apart: 6 -> 7, of which waited for: 6 -> 7; matrix products, arithmetic and copies ran while one was open for 1% -> 1% of each run, Pallas kernels for 0% -> 0%
where the time goes in v1:
time: 1280 us
  waiting for transfers between devices  757 us (59%)
  blocking collectives  438 us (34%)
  between operations  26.3 us (2%)
  matrix products  25.3 us (2%)
  starting transfers between devices  17.7 us (1%)
  other arithmetic  14.8 us (1%)
    psum x6, waiting for transfers between devices, em_map(): c_total, d_total = lax.psum((c_part, d_part), 'ind')  744 us
    psum x3, blocking collectives, per_device(): first, second = lax.psum((first_local, second_local), ('ind', 'snp'))  298 us
    psum x6, blocking collectives, em_map(): sum_a, sum_b = lax.psum((sum_a, sum_b), 'snp')  140 us
  transfers between devices with their start and end apart: 7, of which 7 were waited for; matrix products, arithmetic and copies ran while one was open for 1% of the time, Pallas kernels for 0%

profile of v1, /device:TPU:1, one launch (start us, length us, event | category | flops | bytes accessed | tf_op | source)
XLA Modules:
  0.0 1283.5 jit_solution(10302896450984361995)
XLA Ops:
  7.2 0.8 copy.10
  8.1 1.1 reshape.20
  9.3 17.3 %all-to-all-start = ((f32[64,1,1024]{2,1,0:T(1,128)}), f32[64,1,1024]{2,1,0:T(1,128)S(1)}, u32[]{:S(2)}, u32[]{:S(2)}) async-start(f32[64,1,1024]{2,1,0:T(1,128)} %reshape.20), calls=%async_computation | async-start | bytes 524288 | tf_op jit(solution)/shard_map/all_to_all | solution.py:27
  26.8 12.3 all-to-all-done
  39.1 0.5 broadcast.106
  39.6 1.3 reduce
  41.2 0.6 copy.11
  41.8 0.5 reshape.19
  42.3 0.6 fusion.47
  43.0 1.2 fusion.45
  44.2 1.2 fusion.44
  45.5 0.6 fusion.72
  46.0 0.6 convolution_add_fusion.5
  46.6 23.6 %psum.240 = f32[64,32]{0,1:T(8,128)S(1)} all-reduce(f32[64,32]{0,1:T(8,128)S(1)} %convolution_add_fusion.5), channel_id=1, replica_groups=mesh['ind'=64,'snp'=8] {'snp'}, use_global_device_ids=true, to_apply=%region_1.0 | all-reduce | flops 2048 | bytes 16384 | tf_op jit(solution)/shard_map/psum | solution.py:40
  70.2 122.0 %all-reduce.26.cloned.1.call-done = (f32[2048,32]{0,1:T(8,128)}, f32[2048,32]{0,1:T(8,128)}) async-done(((f32[2048,32]{0,1:T(8,128)}, f32[2048,32]{0,1:T(8,128)}), (f32[2048,32]{0,1:T(8,128)}, f32[2048,32]{0,1:T(8,128)})) %all-reduce.26.cloned.1.call-update) | async-done | bytes 524304 | tf_op jit(solution)/shard_map/psum | solution.py:43
  192.3 1.7 multiply_reduce_fusion.5
  194.0 0.6 fusion.29
  194.6 1.2 fusion.26
  195.8 1.2 fusion.27
  197.1 0.6 fusion.69
  197.7 0.6 convolution_add_fusion.4
  198.3 24.9 %psum.241 = f32[64,32]{0,1:T(8,128)S(1)} all-reduce(f32[64,32]{0,1:T(8,128)S(1)} %convolution_add_fusion.4), channel_id=1, replica_groups=mesh['ind'=64,'snp'=8] {'snp'}, use_global_device_ids=true, to_apply=%region_9.0 | all-reduce | flops 2048 | bytes 16384 | tf_op jit(solution)/shard_map/psum | solution.py:40
  223.2 0.7 multiply_reduce_fusion.10
  225.9 123.8 %all-reduce.24.cloned.1.call-done = (f32[2048,32]{0,1:T(8,128)}, f32[2048,32]{0,1:T(8,128)}) async-done(((f32[2048,32]{0,1:T(8,128)}, f32[2048,32]{0,1:T(8,128)}), (f32[2048,32]{0,1:T(8,128)}, f32[2048,32]{0,1:T(8,128)})) %all-reduce.24.cloned.1.call-update) | async-done | bytes 524304 | tf_op jit(solution)/shard_map/psum | solution.py:43
  349.7 1.7 multiply_reduce_fusion.4
  352.1 99.4 %all-reduce.2 = (f32[]{:T(128)}, f32[]{:T(128)}) all-reduce(f32[]{:T(128)S(6)} %add.164, f32[]{:T(128)S(6)} %add.169), channel_id=1, replica_groups=mesh['ind'=64,'snp'=8] {'ind','snp'}, use_global_device_ids=true, to_apply=%region_8.0 | all-reduce | flops 2 | bytes 16 | tf_op jit(solution)/shard_map/psum | solution.py:56
  452.9 0.6 fusion.51
  453.6 1.2 fusion.48
  454.8 1.2 fusion.49
  456.3 0.6 fusion.66
  456.8 0.6 convolution_add_fusion.3
  457.4 20.8 %psum.242 = f32[64,32]{0,1:T(8,128)S(1)} all-reduce(f32[64,32]{0,1:T(8,128)S(1)} %convolution_add_fusion.3), channel_id=1, replica_groups=mesh['ind'=64,'snp'=8] {'snp'}, use_global_device_ids=true, to_apply=%region_18.19 | all-reduce | flops 2048 | bytes 16384 | tf_op jit(solution)/shard_map/psum | solution.py:40
  478.2 125.2 %all-reduce.22.cloned.1.call-done = (f32[2048,32]{0,1:T(8,128)}, f32[2048,32]{0,1:T(8,128)}) async-done(((f32[2048,32]{0,1:T(8,128)}, f32[2048,32]{0,1:T(8,128)}), (f32[2048,32]{0,1:T(8,128)}, f32[2048,32]{0,1:T(8,128)})) %all-reduce.22.cloned.1.call-update) | async-done | bytes 524304 | tf_op jit(solution)/shard_map/psum | solution.py:43
  603.5 1.7 multiply_reduce_fusion.3
  605.2 0.6 fusion.35
  605.8 1.2 fusion.32
  607.0 1.2 fusion.33
  608.3 0.6 fusion.63
  609.6 0.6 convolution_add_fusion.2
  610.2 24.9 %psum.243 = f32[64,32]{0,1:T(8,128)S(1)} all-reduce(f32[64,32]{0,1:T(8,128)S(1)} %convolution_add_fusion.2), channel_id=1, replica_groups=mesh['ind'=64,'snp'=8] {'snp'}, use_global_device_ids=true, to_apply=%region_26.27 | all-reduce | flops 2048 | bytes 16384 | tf_op jit(solution)/shard_map/psum | solution.py:40
  635.1 0.6 multiply_reduce_fusion.8
  637.0 123.9 %all-reduce.20.cloned.1.call-done = (f32[2048,32]{0,1:T(8,128)}, f32[2048,32]{0,1:T(8,128)}) async-done(((f32[2048,32]{0,1:T(8,128)}, f32[2048,32]{0,1:T(8,128)}), (f32[2048,32]{0,1:T(8,128)}, f32[2048,32]{0,1:T(8,128)})) %all-reduce.20.cloned.1.call-update) | async-done | bytes 524304 | tf_op jit(solution)/shard_map/psum | solution.py:43
  760.9 1.7 multiply_reduce_fusion.2
  763.3 99.4 %all-reduce.1 = (f32[]{:T(128)}, f32[]{:T(128)}) all-reduce(f32[]{:T(128)S(6)} %add.175, f32[]{:T(128)S(6)} %add.180), channel_id=1, replica_groups=mesh['ind'=64,'snp'=8] {'ind','snp'}, use_global_device_ids=true, to_apply=%region_25.26 | all-reduce | flops 2 | bytes 16 | tf_op jit(solution)/shard_map/psum | solution.py:56
  864.1 0.6 fusion.55
  864.7 1.2 fusion.52
  865.9 1.2 fusion.53
  867.2 0.6 fusion.60
  867.8 0.6 convolution_add_fusion.1
  868.4 20.8 %psum.244 = f32[64,32]{0,1:T(8,128)S(1)} all-reduce(f32[64,32]{0,1:T(8,128)S(1)} %convolution_add_fusion.1), channel_id=1, replica_groups=mesh['ind'=64,'snp'=8] {'snp'}, use_global_device_ids=true, to_apply=%region_35.36 | all-reduce | flops 2048 | bytes 16384 | tf_op jit(solution)/shard_map/psum | solution.py:40
  889.2 125.5 %all-reduce.18.cloned.1.call-done = (f32[2048,32]{0,1:T(8,128)}, f32[2048,32]{0,1:T(8,128)}) async-done(((f32[2048,32]{0,1:T(8,128)}, f32[2048,32]{0,1:T(8,128)}), (f32[2048,32]{0,1:T(8,128)}, f32[2048,32]{0,1:T(8,128)})) %all-reduce.18.cloned.1.call-update) | async-done | bytes 524304 | tf_op jit(solution)/shard_map/psum | solution.py:43
  1014.7 1.7 multiply_reduce_fusion.1
  1016.4 0.6 fusion.41
  1017.0 1.2 fusion.39
  1018.2 1.2 fusion.38
  1019.5 0.6 fusion.57
  1020.7 0.6 convolution_add_fusion
  1021.3 24.9 %psum.245 = f32[64,32]{0,1:T(8,128)S(1)} all-reduce(f32[64,32]{0,1:T(8,128)S(1)} %convolution_add_fusion), channel_id=1, replica_groups=mesh['ind'=64,'snp'=8] {'snp'}, use_global_device_ids=true, to_apply=%region_43.44 | all-reduce | flops 2048 | bytes 16384 | tf_op jit(solution)/shard_map/psum | solution.py:40
  1046.2 0.6 multiply_reduce_fusion.6
  1048.2 123.9 %all-reduce.16.cloned.1.call-done = (f32[2048,32]{0,1:T(8,128)}, f32[2048,32]{0,1:T(8,128)}) async-done(((f32[2048,32]{0,1:T(8,128)}, f32[2048,32]{0,1:T(8,128)}), (f32[2048,32]{0,1:T(8,128)}, f32[2048,32]{0,1:T(8,128)})) %all-reduce.16.cloned.1.call-update) | async-done | bytes 524304 | tf_op jit(solution)/shard_map/psum | solution.py:43
  1172.1 1.7 multiply_reduce_fusion
  1174.5 99.4 %all-reduce = (f32[]{:T(128)}, f32[]{:T(128)}) all-reduce(f32[]{:T(128)S(6)} %add.186, f32[]{:T(128)S(6)} %add.191), channel_id=1, replica_groups=mesh['ind'=64,'snp'=8] {'ind','snp'}, use_global_device_ids=true, to_apply=%region_42.43 | all-reduce | flops 2 | bytes 16 | tf_op jit(solution)/shard_map/psum | solution.py:56
  1275.3 0.7 copy.12
  1276.0 0.6 broadcast_divide_fusion
  (34 shorter events, 1.6 us)
Async XLA Ops:
  8.1 18.5 %copy-start.2 = (f32[64,32]{0,1:T(8,128)S(1)}, f32[64,32]{0,1:T(8,128)}, u32[]{:S(2)}) copy-start(f32[64,32]{0,1:T(8,128)} %param.6) | copy-start | bytes 24580
  8.1 18.5 %copy-start.1 = (s32[64,2048]{1,0:T(8,128)S(1)}, s32[64,2048]{1,0:T(8,128)}, u32[]{:S(2)}) copy-start(s32[64,2048]{1,0:T(8,128)} %param.5) | copy-start | bytes 1572868
  9.3 17.4 %copy-start = (s32[64,2048]{1,0:T(8,128)S(1)}, s32[64,2048]{1,0:T(8,128)}, u32[]{:S(2)}) copy-start(s32[64,2048]{1,0:T(8,128)} %param.4) | copy-start | bytes 1572868
  9.3 29.8 %all-to-all-start = ((f32[64,1,1024]{2,1,0:T(1,128)}), f32[64,1,1024]{2,1,0:T(1,128)S(1)}, u32[]{:S(2)}, u32[]{:S(2)}) async-start(f32[64,1,1024]{2,1,0:T(1,128)} %reshape.20), calls=%async_computation | async-start | bytes 524288 | tf_op jit(solution)/shard_map/all_to_all | solution.py:27
  26.5 165.7 %all-reduce.26.cloned.1.call-start = ((), (), s32[]{:S(2)}) async-start(), calls=%async_computation.6 | async-start | bytes 1048576 | tf_op jit(solution)/shard_map/psum | solution.py:43
  45.4 304.3 %all-reduce.24.cloned.1.call-start = ((), (), s32[]{:S(2)}) async-start(), calls=%async_computation.5 | async-start | bytes 1048576 | tf_op jit(solution)/shard_map/psum | solution.py:43
  197.1 406.4 %all-reduce.22.cloned.1.call-start = ((), (), s32[]{:S(2)}) async-start(), calls=%async_computation.4 | async-start | bytes 1048576 | tf_op jit(solution)/shard_map/psum | solution.py:43
  456.0 304.9 %all-reduce.20.cloned.1.call-start = ((), (), s32[]{:S(2)}) async-start(), calls=%async_computation.3 | async-start | bytes 1048576 | tf_op jit(solution)/shard_map/psum | solution.py:43
  608.3 406.4 %all-reduce.18.cloned.1.call-start = ((), (), s32[]{:S(2)}) async-start(), calls=%async_computation.2 | async-start | bytes 1048576 | tf_op jit(solution)/shard_map/psum | solution.py:43
  867.2 304.9 %all-reduce.16.cloned.1.call-start = ((), (), s32[]{:S(2)}) async-start(), calls=%async_computation.1 | async-start | bytes 1048576 | tf_op jit(solution)/shard_map/psum | solution.py:43
Sparse Core Ops, SparseCore 0:
  45.5 146.6 all-reduce.25
  197.2 152.5 all-reduce.23
  456.1 147.2 all-reduce.21
  608.4 152.4 all-reduce.19
  867.3 147.3 all-reduce.17
  1019.6 152.4 all-reduce.15
